TPU v7x, 512 devices: a whole 4x4x16 slice. The times are simulated.
512 devices in a mesh: pipe: 16 (over z), seq: 8 (over y, core), dp: 4 (over x).
Axes of the slice: x: 4, y: 4, z: 16, core: 2. Of those that a mesh axis runs over, the one named last changes fastest.
Arguments:
- acts: bfloat16 [16, 4, 1024, 8192], P('pipe', 'dp', 'seq'), may hold values from -6 to 6
- top_grad: bfloat16 [4, 1024, 8192], P('dp', 'seq'), may hold values from -6 to 6
- a_rows: bfloat16 [16, 32, 8192], P('pipe', None, ('seq', 'dp')), may hold values from -1 to 1
- b_rows: bfloat16 [16, 32, 8192], P('pipe', None, ('seq', 'dp')), may hold values from -0.375 to 0.375
- gain: bfloat16 [16, 8192], P('pipe', ('seq', 'dp')), may hold values from 0.5 to 1.5
Outputs:
- grad_a: float32 [16, 32, 8192], P('pipe', None, ('seq', 'dp'))
- grad_b: float32 [16, 32, 8192], P('pipe', None, ('seq', 'dp'))
- grad_gain: float32 [16, 8192], P('pipe', ('seq', 'dp'))
- clip_factors: float32 [4], P('dp')
All inputs are finite; a program needn't handle non-finite values.
Results may differ from a plain program's by a relative error of at most 0.019.
Values may be sent and summed in bfloat16 or wider, within the bound.
No kernel may reach another device: no remote copies, remote signals or barrier semaphores. Data moves between devices by JAX's collectives and lax.ppermute only.
A program may use at most 64 MiB of HBM per device.

v0:
```python
import math
import jax
import jax.numpy as jnp
from jax import lax
from jax.sharding import PartitionSpec as P

rows_per_block = 32


def from_behind(value, axis, steps):
    count = lax.axis_size(axis)
    initial, last = (max(0, -steps), min(count, count - steps))
    return lax.ppermute(value, axis, [(source, source + steps) for source in range(initial, last)])


def on_device(acts, top_grad, a_rows, b_rows, gain):
    sections = lax.axis_size("pipe")
    section = lax.axis_index("pipe")
    hidden = acts[0, 0]
    top = top_grad[0]
    a_whole, b_whole, gain_whole = (
        lax.all_gather(a_rows, ("seq", "dp"), axis=2, tiled=True),
        lax.all_gather(b_rows, ("seq", "dp"), axis=2, tiled=True),
        lax.all_gather(gain[:, None, :], ("seq", "dp"), axis=2, tiled=True),
    )
    a_full = a_whole[0]
    b_full = b_whole[0]
    gain_float = gain_whole[0, 0].astype(jnp.float32)
    rows, width = hidden.shape
    rank = a_full.shape[0]
    block_total = rows // rows_per_block
    hidden_float = hidden.astype(jnp.float32)
    inverse_root_mean = jnp.sqrt(
        jnp.mean(hidden_float * hidden_float, axis=-1, keepdims=True) + 1e-05
    )
    input_normalized = hidden_float / inverse_root_mean
    normalized_rows = (input_normalized * gain_float).astype(jnp.bfloat16)
    low = jnp.dot(normalized_rows, a_full.T, preferred_element_type=jnp.float32).astype(
        jnp.bfloat16
    )
    contract_last = (((1,), (1,)), ((), ()))
    contract_first = (((0,), (0,)), ((), ()))

    def back_block(upstream_gradient, block_offset):
        input_portion = lax.dynamic_slice_in_dim(input_normalized, block_offset, rows_per_block, 0)
        r_part = lax.dynamic_slice_in_dim(inverse_root_mean, block_offset, rows_per_block, 0)
        d_low = lax.dot_general(
            upstream_gradient, b_full, contract_last, preferred_element_type=jnp.float32
        ).astype(jnp.bfloat16)
        normalized_gradient = jnp.dot(d_low, a_full, preferred_element_type=jnp.float32)
        input_gradient = normalized_gradient * gain_float
        hidden_gradient = (
            upstream_gradient.astype(jnp.float32)
            + (
                input_gradient
                - input_portion * jnp.mean(input_gradient * input_portion, axis=-1, keepdims=True)
            )
            / r_part
        )
        return hidden_gradient.astype(jnp.bfloat16)

    def turn(turn_index, carry):
        incoming, mine = carry
        block_index = turn_index - (sections - 1 - section)
        inside = jnp.logical_and(block_index >= 0, block_index < block_total)
        block_offset = jnp.clip(block_index, 0, block_total - 1) * rows_per_block
        top_block = lax.dynamic_slice_in_dim(top, block_offset, rows_per_block, 0)
        source = jnp.where(section == sections - 1, top_block, incoming)
        kept = lax.dynamic_slice_in_dim(mine, block_offset, rows_per_block, 0)
        mine = lax.dynamic_update_slice_in_dim(
            mine, jnp.where(inside, source, kept), block_offset, 0
        )
        result = back_block(source, block_offset)
        incoming = from_behind(result, "pipe", -1)
        return (incoming, mine)

    begin = (
        jnp.zeros((rows_per_block, width), jnp.bfloat16),
        jnp.zeros((rows, width), jnp.bfloat16),
    )
    mine = lax.fori_loop(0, sections + block_total - 1, turn, begin)[1]
    d_low = lax.dot_general(mine, b_full, contract_last, preferred_element_type=jnp.float32).astype(
        jnp.bfloat16
    )
    normalized_gradient = jnp.dot(d_low, a_full, preferred_element_type=jnp.float32)
    grad_a = lax.dot_general(
        d_low, normalized_rows, contract_first, preferred_element_type=jnp.float32
    )
    grad_b = lax.dot_general(low, mine, contract_first, preferred_element_type=jnp.float32)
    gain_gradient = jnp.sum(normalized_gradient * input_normalized, axis=0)[None, :]
    grad_a, grad_b, gain_gradient = (grad_a, grad_b, gain_gradient)
    sum_a, sum_b, sum_g = lax.psum((grad_a, grad_b, gain_gradient), "seq")
    square = jnp.sum(sum_a * sum_a) + jnp.sum(sum_b * sum_b) + jnp.sum(sum_g * sum_g)
    total = lax.psum(square, "pipe")
    share = width // lax.axis_size("seq")
    offset = lax.axis_index("seq") * share
    part_a = lax.dynamic_slice_in_dim(sum_a, offset, share, 1)
    part_b = lax.dynamic_slice_in_dim(sum_b, offset, share, 1)
    part_g = lax.dynamic_slice_in_dim(sum_g, offset, share, 1)
    bound = math.sqrt(sections * (2 * rank + 1) * width)
    factor = bound / (jnp.sqrt(total) + 0.01 * bound)
    out_a, out_b, out_g = (
        lax.psum_scatter(factor * part_a, "dp", scatter_dimension=1, tiled=True),
        lax.psum_scatter(factor * part_b, "dp", scatter_dimension=1, tiled=True),
        lax.psum_scatter(factor * part_g, "dp", scatter_dimension=1, tiled=True),
    )
    return (out_a[None], out_b[None], out_g, jnp.reshape(factor, (1,)))


def solution(mesh):
    in_specs = (
        P("pipe", "dp", "seq", None),
        P("dp", "seq", None),
        P("pipe", None, ("seq", "dp")),
        P("pipe", None, ("seq", "dp")),
        P("pipe", ("seq", "dp")),
    )
    out_specs = (
        P("pipe", None, ("seq", "dp")),
        P("pipe", None, ("seq", "dp")),
        P("pipe", ("seq", "dp")),
        P("dp"),
    )
    return jax.shard_map(
        on_device, mesh=mesh, in_specs=in_specs, out_specs=out_specs, check_vma=False
    )
```

profile of v0, /device:TPU:8, one launch (start us, length us, event | category | flops | bytes accessed | tf_op | source)
XLA Modules:
  0.0 737.9 jit_solution(11694105464308485738)
XLA Ops:
  7.2 2.2 fusion.3
  9.5 2.4 fusion.1
  11.9 35.9 %all_gather.10 = bf16[1,32,8192]{2,1,0:T(8,128)(2,1)S(1)} all-gather(bf16[1,32,256]{2,1,0:T(8,128)(2,1)S(1)} %copy-done.2), channel_id=1, replica_groups=mesh['pipe'=16,'seq'=8,'dp'=4] {'seq','dp'}, dimensions={2}, use_global_device_ids=true | all-gather | bytes 540672 | tf_op jit(solution)/shard_map/all_gather | solution.py:22
  47.8 34.2 %all-gather = bf16[1,8192]{1,0:T(2,128)(2,1)S(1)} all-gather(bf16[1,256]{1,0:T(2,128)(2,1)S(1)} %copy-done.4), channel_id=2, replica_groups=mesh['pipe'=16,'seq'=8,'dp'=4] {'seq','dp'}, dimensions={1}, use_global_device_ids=true | all-gather | bytes 16896 | tf_op jit(solution)/shard_map/all_gather | solution.py:24
  82.1 32.9 %all_gather.9 = bf16[1,32,8192]{2,1,0:T(8,128)(2,1)S(1)} all-gather(bf16[1,32,256]{2,1,0:T(8,128)(2,1)S(1)} %copy-done.3), channel_id=1, replica_groups=mesh['pipe'=16,'seq'=8,'dp'=4] {'seq','dp'}, dimensions={2}, use_global_device_ids=true | all-gather | bytes 540672 | tf_op jit(solution)/shard_map/all_gather | solution.py:23
  116.6 392.1 %while.17 = (s32[]{:T(128)}, bf16[32,8192]{1,0:T(8,128)(2,1)S(1)}, bf16[128,8192]{1,0:T(8,128)(2,1)}, pred[]{:T(512)}, s32[]{:T(128)}, /*index=5*/bf16[128,8192]...) while((s32[]{:T(128)}, bf16[32,8192]{1,0:T(8,128)(2,1)S(1)}, ...), condition=%wide.region_3.4_spmd, body=%wide.region_1.3_spmd.sunk | while | flops 36439052 | bytes 11568829 | solution.py:81
  116.6 2.2 select_dynamic-update-slice_fusion.2
  121.0 2.3 add_convert_fusion.2
  124.6 14.6 %collective-permute-done = bf16[32,8192]{1,0:T(8,128)(2,1)S(1)} collective-permute-done((bf16[32,8192]{1,0:T(8,128)(2,1)}, bf16[32,8192]{1,0:T(8,128)(2,1)S(1)}, u32[]{:S(2)}, u32[]{:S(2)}) %collective-permute-start) | collective-permute-done | bytes 524320 | tf_op jit(solution)/shard_map/while/body/eval_jaxpr/ppermute | solution.py:13
  139.2 2.2 select_dynamic-update-slice_fusion.2
  143.6 2.3 add_convert_fusion.2
  147.2 13.7 %collective-permute-done = bf16[32,8192]{1,0:T(8,128)(2,1)S(1)} collective-permute-done((bf16[32,8192]{1,0:T(8,128)(2,1)}, bf16[32,8192]{1,0:T(8,128)(2,1)S(1)}, u32[]{:S(2)}, u32[]{:S(2)}) %collective-permute-start) | collective-permute-done | bytes 524320 | tf_op jit(solution)/shard_map/while/body/eval_jaxpr/ppermute | solution.py:13
  160.9 2.2 select_dynamic-update-slice_fusion.2
  165.3 2.3 add_convert_fusion.2
  168.9 12.9 %collective-permute-done = bf16[32,8192]{1,0:T(8,128)(2,1)S(1)} collective-permute-done((bf16[32,8192]{1,0:T(8,128)(2,1)}, bf16[32,8192]{1,0:T(8,128)(2,1)S(1)}, u32[]{:S(2)}, u32[]{:S(2)}) %collective-permute-start) | collective-permute-done | bytes 524320 | tf_op jit(solution)/shard_map/while/body/eval_jaxpr/ppermute | solution.py:13
  186.2 2.3 add_convert_fusion.2
  189.7 12.0 %collective-permute-done = bf16[32,8192]{1,0:T(8,128)(2,1)S(1)} collective-permute-done((bf16[32,8192]{1,0:T(8,128)(2,1)}, bf16[32,8192]{1,0:T(8,128)(2,1)S(1)}, u32[]{:S(2)}, u32[]{:S(2)}) %collective-permute-start) | collective-permute-done | bytes 524320 | tf_op jit(solution)/shard_map/while/body/eval_jaxpr/ppermute | solution.py:13
  201.8 2.2 select_dynamic-update-slice_fusion.2
  206.2 2.3 add_convert_fusion.2
  209.8 12.6 %collective-permute-done = bf16[32,8192]{1,0:T(8,128)(2,1)S(1)} collective-permute-done((bf16[32,8192]{1,0:T(8,128)(2,1)}, bf16[32,8192]{1,0:T(8,128)(2,1)S(1)}, u32[]{:S(2)}, u32[]{:S(2)}) %collective-permute-start) | collective-permute-done | bytes 524320 | tf_op jit(solution)/shard_map/while/body/eval_jaxpr/ppermute | solution.py:13
  222.3 2.2 select_dynamic-update-slice_fusion.2
  226.7 2.3 add_convert_fusion.2
  230.3 11.7 %collective-permute-done = bf16[32,8192]{1,0:T(8,128)(2,1)S(1)} collective-permute-done((bf16[32,8192]{1,0:T(8,128)(2,1)}, bf16[32,8192]{1,0:T(8,128)(2,1)S(1)}, u32[]{:S(2)}, u32[]{:S(2)}) %collective-permute-start) | collective-permute-done | bytes 524320 | tf_op jit(solution)/shard_map/while/body/eval_jaxpr/ppermute | solution.py:13
  242.0 2.2 select_dynamic-update-slice_fusion.2
  246.4 2.3 add_convert_fusion.2
  250.0 10.8 %collective-permute-done = bf16[32,8192]{1,0:T(8,128)(2,1)S(1)} collective-permute-done((bf16[32,8192]{1,0:T(8,128)(2,1)}, bf16[32,8192]{1,0:T(8,128)(2,1)S(1)}, u32[]{:S(2)}, u32[]{:S(2)}) %collective-permute-start) | collective-permute-done | bytes 524320 | tf_op jit(solution)/shard_map/while/body/eval_jaxpr/ppermute | solution.py:13
  260.8 2.2 select_dynamic-update-slice_fusion.2
  265.2 2.3 add_convert_fusion.2
  268.8 10.4 %collective-permute-done = bf16[32,8192]{1,0:T(8,128)(2,1)S(1)} collective-permute-done((bf16[32,8192]{1,0:T(8,128)(2,1)}, bf16[32,8192]{1,0:T(8,128)(2,1)S(1)}, u32[]{:S(2)}, u32[]{:S(2)}) %collective-permute-start) | collective-permute-done | bytes 524320 | tf_op jit(solution)/shard_map/while/body/eval_jaxpr/ppermute | solution.py:13
  283.6 2.3 add_convert_fusion.2
  287.2 10.7 %collective-permute-done = bf16[32,8192]{1,0:T(8,128)(2,1)S(1)} collective-permute-done((bf16[32,8192]{1,0:T(8,128)(2,1)}, bf16[32,8192]{1,0:T(8,128)(2,1)S(1)}, u32[]{:S(2)}, u32[]{:S(2)}) %collective-permute-start) | collective-permute-done | bytes 524320 | tf_op jit(solution)/shard_map/while/body/eval_jaxpr/ppermute | solution.py:13
  302.3 2.3 add_convert_fusion.2
  305.9 11.2 %collective-permute-done = bf16[32,8192]{1,0:T(8,128)(2,1)S(1)} collective-permute-done((bf16[32,8192]{1,0:T(8,128)(2,1)}, bf16[32,8192]{1,0:T(8,128)(2,1)S(1)}, u32[]{:S(2)}, u32[]{:S(2)}) %collective-permute-start) | collective-permute-done | bytes 524320 | tf_op jit(solution)/shard_map/while/body/eval_jaxpr/ppermute | solution.py:13
  321.5 2.3 add_convert_fusion.2
  325.0 11.2 %collective-permute-done = bf16[32,8192]{1,0:T(8,128)(2,1)S(1)} collective-permute-done((bf16[32,8192]{1,0:T(8,128)(2,1)}, bf16[32,8192]{1,0:T(8,128)(2,1)S(1)}, u32[]{:S(2)}, u32[]{:S(2)}) %collective-permute-start) | collective-permute-done | bytes 524320 | tf_op jit(solution)/shard_map/while/body/eval_jaxpr/ppermute | solution.py:13
  340.6 2.3 add_convert_fusion.2
  344.2 11.2 %collective-permute-done = bf16[32,8192]{1,0:T(8,128)(2,1)S(1)} collective-permute-done((bf16[32,8192]{1,0:T(8,128)(2,1)}, bf16[32,8192]{1,0:T(8,128)(2,1)S(1)}, u32[]{:S(2)}, u32[]{:S(2)}) %collective-permute-start) | collective-permute-done | bytes 524320 | tf_op jit(solution)/shard_map/while/body/eval_jaxpr/ppermute | solution.py:13
  359.8 2.3 add_convert_fusion.2
  363.4 11.2 %collective-permute-done = bf16[32,8192]{1,0:T(8,128)(2,1)S(1)} collective-permute-done((bf16[32,8192]{1,0:T(8,128)(2,1)}, bf16[32,8192]{1,0:T(8,128)(2,1)S(1)}, u32[]{:S(2)}, u32[]{:S(2)}) %collective-permute-start) | collective-permute-done | bytes 524320 | tf_op jit(solution)/shard_map/while/body/eval_jaxpr/ppermute | solution.py:13
  379.0 2.3 add_convert_fusion.2
  382.6 11.9 %collective-permute-done = bf16[32,8192]{1,0:T(8,128)(2,1)S(1)} collective-permute-done((bf16[32,8192]{1,0:T(8,128)(2,1)}, bf16[32,8192]{1,0:T(8,128)(2,1)S(1)}, u32[]{:S(2)}, u32[]{:S(2)}) %collective-permute-start) | collective-permute-done | bytes 524320 | tf_op jit(solution)/shard_map/while/body/eval_jaxpr/ppermute | solution.py:13
  398.9 2.3 add_convert_fusion.2
  402.5 13.4 %collective-permute-done = bf16[32,8192]{1,0:T(8,128)(2,1)S(1)} collective-permute-done((bf16[32,8192]{1,0:T(8,128)(2,1)}, bf16[32,8192]{1,0:T(8,128)(2,1)S(1)}, u32[]{:S(2)}, u32[]{:S(2)}) %collective-permute-start) | collective-permute-done | bytes 524320 | tf_op jit(solution)/shard_map/while/body/eval_jaxpr/ppermute | solution.py:13
  420.3 2.3 add_convert_fusion.2
  423.9 15.3 %collective-permute-done = bf16[32,8192]{1,0:T(8,128)(2,1)S(1)} collective-permute-done((bf16[32,8192]{1,0:T(8,128)(2,1)}, bf16[32,8192]{1,0:T(8,128)(2,1)S(1)}, u32[]{:S(2)}, u32[]{:S(2)}) %collective-permute-start) | collective-permute-done | bytes 524320 | tf_op jit(solution)/shard_map/while/body/eval_jaxpr/ppermute | solution.py:13
  439.2 2.2 select_dynamic-update-slice_fusion.2
  443.6 2.3 add_convert_fusion.2
  447.2 16.1 %collective-permute-done = bf16[32,8192]{1,0:T(8,128)(2,1)S(1)} collective-permute-done((bf16[32,8192]{1,0:T(8,128)(2,1)}, bf16[32,8192]{1,0:T(8,128)(2,1)S(1)}, u32[]{:S(2)}, u32[]{:S(2)}) %collective-permute-start) | collective-permute-done | bytes 524320 | tf_op jit(solution)/shard_map/while/body/eval_jaxpr/ppermute | solution.py:13
  463.3 2.2 select_dynamic-update-slice_fusion.2
  467.7 2.3 add_convert_fusion.2
  471.3 17.4 %collective-permute-done = bf16[32,8192]{1,0:T(8,128)(2,1)S(1)} collective-permute-done((bf16[32,8192]{1,0:T(8,128)(2,1)}, bf16[32,8192]{1,0:T(8,128)(2,1)S(1)}, u32[]{:S(2)}, u32[]{:S(2)}) %collective-permute-start) | collective-permute-done | bytes 524320 | tf_op jit(solution)/shard_map/while/body/eval_jaxpr/ppermute | solution.py:13
  488.7 2.2 select_dynamic-update-slice_fusion.2
  493.1 2.3 add_convert_fusion.2
  496.7 12.0 %collective-permute-done = bf16[32,8192]{1,0:T(8,128)(2,1)S(1)} collective-permute-done((bf16[32,8192]{1,0:T(8,128)(2,1)}, bf16[32,8192]{1,0:T(8,128)(2,1)S(1)}, u32[]{:S(2)}, u32[]{:S(2)}) %collective-permute-start) | collective-permute-done | bytes 524320 | tf_op jit(solution)/shard_map/while/body/eval_jaxpr/ppermute | solution.py:13
  508.7 4.9 fusion.16
  513.6 2.5 convolution_convert_fusion.1
  518.1 2.4 fusion.11
  520.5 23.2 %psum.30 = f32[1,8192]{1,0:T(1,128)S(1)} all-reduce(f32[1,8192]{1,0:T(1,128)S(1)} %bitcast.65), channel_id=1, replica_groups=mesh['pipe'=16,'seq'=8,'dp'=4] {'seq'}, use_global_device_ids=true, to_apply=%region_9.10 | all-reduce | flops 8192 | bytes 65536 | tf_op jit(solution)/shard_map/psum | solution.py:92
  544.4 57.9 %all-reduce.3.cloned.1.call-done = (f32[32,8192]{1,0:T(8,128)}, f32[32,8192]{1,0:T(8,128)}) async-done(((f32[32,8192]{1,0:T(8,128)}, f32[32,8192]{1,0:T(8,128)}), (f32[32,8192]{1,0:T(8,128)}, f32[32,8192]{1,0:T(8,128)})) %all-reduce.3.cloned.1.call-update) | async-done | bytes 2097168 | tf_op jit(solution)/shard_map/psum | solution.py:92
  602.3 2.4 multiply_reduce_fusion.1
  606.7 31.8 %psum.31 = f32[]{:T(128)} all-reduce(f32[]{:T(128)S(6)} %add.88), channel_id=1, replica_groups=mesh['pipe'=16,'seq'=8,'dp'=4] {'pipe'}, use_global_device_ids=true, to_apply=%region_11.12 | all-reduce | flops 1 | bytes 8 | tf_op jit(solution)/shard_map/psum | solution.py:94
  643.5 23.8 %reduce-scatter.10.cloned.1.call-done = f32[256,1]{1,0:T(8,128)} async-done(((f32[1024,1]{1,0:T(8,128)}), f32[256,1]{1,0:T(8,128)}) %reduce-scatter.10.cloned.1.call-update) | async-done | bytes 1040
  668.9 30.0 %reduce-scatter.8.cloned.1.call-done = f32[32,256]{1,0:T(8,128)} async-done(((f32[32,1024]{1,0:T(8,128)}), f32[32,256]{1,0:T(8,128)}) %reduce-scatter.8.cloned.1.call-update) | async-done | bytes 32784 | tf_op jit(solution)/shard_map/reduce_scatter | solution.py:104
  698.9 31.4 %reduce-scatter.6.cloned.1.call-done = f32[32,256]{1,0:T(8,128)} async-done(((f32[32,1024]{1,0:T(8,128)}), f32[32,256]{1,0:T(8,128)}) %reduce-scatter.6.cloned.1.call-update) | async-done | bytes 32784 | tf_op jit(solution)/shard_map/reduce_scatter | solution.py:103
  (114 shorter events, 95.9 us)
Async XLA Ops:
  7.2 595.1 %all-reduce.3.cloned.1.call-start = ((), (), s32[]{:S(2)}) async-start(), calls=%async_computation.6 | async-start | bytes 4194304 | tf_op jit(solution)/shard_map/psum | solution.py:92
  7.2 2.3 copy-start
  9.5 2.4 copy-start.2
  9.5 38.4 %copy-start.4 = (bf16[1,256]{1,0:T(2,128)(2,1)S(1)}, bf16[1,256]{1,0:T(2,128)(2,1)}, u32[]{:S(2)}) copy-start(bf16[1,256]{1,0:T(2,128)(2,1)} %param.11) | copy-start | bytes 1540
  9.5 72.6 %copy-start.3 = (bf16[1,32,256]{2,1,0:T(8,128)(2,1)S(1)}, bf16[1,32,256]{2,1,0:T(8,128)(2,1)}, u32[]{:S(2)}) copy-start(bf16[1,32,256]{2,1,0:T(8,128)(2,1)} %param.10) | copy-start | bytes 49156
  123.3 15.9 %collective-permute-start = (bf16[32,8192]{1,0:T(8,128)(2,1)}, bf16[32,8192]{1,0:T(8,128)(2,1)S(1)}, u32[]{:S(2)}, u32[]{:S(2)}) collective-permute-start(bf16[32,8192]{1,0:T(8,128)(2,1)} %add_convert_fusion.2), channel_id=1, source_target_pairs={{32,0},{64,32},{96,64},{128,96},{160,128},{192,160},{224,192},{256... | collective-permute-start | bytes 1572872 | tf_op jit(solution)/shard_map/while/body/eval_jaxpr/ppermute | solution.py:13
  145.9 15.0 %collective-permute-start = (bf16[32,8192]{1,0:T(8,128)(2,1)}, bf16[32,8192]{1,0:T(8,128)(2,1)S(1)}, u32[]{:S(2)}, u32[]{:S(2)}) collective-permute-start(bf16[32,8192]{1,0:T(8,128)(2,1)} %add_convert_fusion.2), channel_id=1, source_target_pairs={{32,0},{64,32},{96,64},{128,96},{160,128},{192,160},{224,192},{256... | collective-permute-start | bytes 1572872 | tf_op jit(solution)/shard_map/while/body/eval_jaxpr/ppermute | solution.py:13
  167.6 14.2 %collective-permute-start = (bf16[32,8192]{1,0:T(8,128)(2,1)}, bf16[32,8192]{1,0:T(8,128)(2,1)S(1)}, u32[]{:S(2)}, u32[]{:S(2)}) collective-permute-start(bf16[32,8192]{1,0:T(8,128)(2,1)} %add_convert_fusion.2), channel_id=1, source_target_pairs={{32,0},{64,32},{96,64},{128,96},{160,128},{192,160},{224,192},{256... | collective-permute-start | bytes 1572872 | tf_op jit(solution)/shard_map/while/body/eval_jaxpr/ppermute | solution.py:13
  188.5 13.3 %collective-permute-start = (bf16[32,8192]{1,0:T(8,128)(2,1)}, bf16[32,8192]{1,0:T(8,128)(2,1)S(1)}, u32[]{:S(2)}, u32[]{:S(2)}) collective-permute-start(bf16[32,8192]{1,0:T(8,128)(2,1)} %add_convert_fusion.2), channel_id=1, source_target_pairs={{32,0},{64,32},{96,64},{128,96},{160,128},{192,160},{224,192},{256... | collective-permute-start | bytes 1572872 | tf_op jit(solution)/shard_map/while/body/eval_jaxpr/ppermute | solution.py:13
  208.5 13.8 %collective-permute-start = (bf16[32,8192]{1,0:T(8,128)(2,1)}, bf16[32,8192]{1,0:T(8,128)(2,1)S(1)}, u32[]{:S(2)}, u32[]{:S(2)}) collective-permute-start(bf16[32,8192]{1,0:T(8,128)(2,1)} %add_convert_fusion.2), channel_id=1, source_target_pairs={{32,0},{64,32},{96,64},{128,96},{160,128},{192,160},{224,192},{256... | collective-permute-start | bytes 1572872 | tf_op jit(solution)/shard_map/while/body/eval_jaxpr/ppermute | solution.py:13
  229.0 13.0 %collective-permute-start = (bf16[32,8192]{1,0:T(8,128)(2,1)}, bf16[32,8192]{1,0:T(8,128)(2,1)S(1)}, u32[]{:S(2)}, u32[]{:S(2)}) collective-permute-start(bf16[32,8192]{1,0:T(8,128)(2,1)} %add_convert_fusion.2), channel_id=1, source_target_pairs={{32,0},{64,32},{96,64},{128,96},{160,128},{192,160},{224,192},{256... | collective-permute-start | bytes 1572872 | tf_op jit(solution)/shard_map/while/body/eval_jaxpr/ppermute | solution.py:13
  248.7 12.1 %collective-permute-start = (bf16[32,8192]{1,0:T(8,128)(2,1)}, bf16[32,8192]{1,0:T(8,128)(2,1)S(1)}, u32[]{:S(2)}, u32[]{:S(2)}) collective-permute-start(bf16[32,8192]{1,0:T(8,128)(2,1)} %add_convert_fusion.2), channel_id=1, source_target_pairs={{32,0},{64,32},{96,64},{128,96},{160,128},{192,160},{224,192},{256... | collective-permute-start | bytes 1572872 | tf_op jit(solution)/shard_map/while/body/eval_jaxpr/ppermute | solution.py:13
  267.5 11.6 %collective-permute-start = (bf16[32,8192]{1,0:T(8,128)(2,1)}, bf16[32,8192]{1,0:T(8,128)(2,1)S(1)}, u32[]{:S(2)}, u32[]{:S(2)}) collective-permute-start(bf16[32,8192]{1,0:T(8,128)(2,1)} %add_convert_fusion.2), channel_id=1, source_target_pairs={{32,0},{64,32},{96,64},{128,96},{160,128},{192,160},{224,192},{256... | collective-permute-start | bytes 1572872 | tf_op jit(solution)/shard_map/while/body/eval_jaxpr/ppermute | solution.py:13
  285.9 12.0 %collective-permute-start = (bf16[32,8192]{1,0:T(8,128)(2,1)}, bf16[32,8192]{1,0:T(8,128)(2,1)S(1)}, u32[]{:S(2)}, u32[]{:S(2)}) collective-permute-start(bf16[32,8192]{1,0:T(8,128)(2,1)} %add_convert_fusion.2), channel_id=1, source_target_pairs={{32,0},{64,32},{96,64},{128,96},{160,128},{192,160},{224,192},{256... | collective-permute-start | bytes 1572872 | tf_op jit(solution)/shard_map/while/body/eval_jaxpr/ppermute | solution.py:13
  304.6 12.5 %collective-permute-start = (bf16[32,8192]{1,0:T(8,128)(2,1)}, bf16[32,8192]{1,0:T(8,128)(2,1)S(1)}, u32[]{:S(2)}, u32[]{:S(2)}) collective-permute-start(bf16[32,8192]{1,0:T(8,128)(2,1)} %add_convert_fusion.2), channel_id=1, source_target_pairs={{32,0},{64,32},{96,64},{128,96},{160,128},{192,160},{224,192},{256... | collective-permute-start | bytes 1572872 | tf_op jit(solution)/shard_map/while/body/eval_jaxpr/ppermute | solution.py:13
  323.7 12.5 %collective-permute-start = (bf16[32,8192]{1,0:T(8,128)(2,1)}, bf16[32,8192]{1,0:T(8,128)(2,1)S(1)}, u32[]{:S(2)}, u32[]{:S(2)}) collective-permute-start(bf16[32,8192]{1,0:T(8,128)(2,1)} %add_convert_fusion.2), channel_id=1, source_target_pairs={{32,0},{64,32},{96,64},{128,96},{160,128},{192,160},{224,192},{256... | collective-permute-start | bytes 1572872 | tf_op jit(solution)/shard_map/while/body/eval_jaxpr/ppermute | solution.py:13
  342.9 12.5 %collective-permute-start = (bf16[32,8192]{1,0:T(8,128)(2,1)}, bf16[32,8192]{1,0:T(8,128)(2,1)S(1)}, u32[]{:S(2)}, u32[]{:S(2)}) collective-permute-start(bf16[32,8192]{1,0:T(8,128)(2,1)} %add_convert_fusion.2), channel_id=1, source_target_pairs={{32,0},{64,32},{96,64},{128,96},{160,128},{192,160},{224,192},{256... | collective-permute-start | bytes 1572872 | tf_op jit(solution)/shard_map/while/body/eval_jaxpr/ppermute | solution.py:13
  362.1 12.5 %collective-permute-start = (bf16[32,8192]{1,0:T(8,128)(2,1)}, bf16[32,8192]{1,0:T(8,128)(2,1)S(1)}, u32[]{:S(2)}, u32[]{:S(2)}) collective-permute-start(bf16[32,8192]{1,0:T(8,128)(2,1)} %add_convert_fusion.2), channel_id=1, source_target_pairs={{32,0},{64,32},{96,64},{128,96},{160,128},{192,160},{224,192},{256... | collective-permute-start | bytes 1572872 | tf_op jit(solution)/shard_map/while/body/eval_jaxpr/ppermute | solution.py:13
  381.3 13.2 %collective-permute-start = (bf16[32,8192]{1,0:T(8,128)(2,1)}, bf16[32,8192]{1,0:T(8,128)(2,1)S(1)}, u32[]{:S(2)}, u32[]{:S(2)}) collective-permute-start(bf16[32,8192]{1,0:T(8,128)(2,1)} %add_convert_fusion.2), channel_id=1, source_target_pairs={{32,0},{64,32},{96,64},{128,96},{160,128},{192,160},{224,192},{256... | collective-permute-start | bytes 1572872 | tf_op jit(solution)/shard_map/while/body/eval_jaxpr/ppermute | solution.py:13
  401.2 14.7 %collective-permute-start = (bf16[32,8192]{1,0:T(8,128)(2,1)}, bf16[32,8192]{1,0:T(8,128)(2,1)S(1)}, u32[]{:S(2)}, u32[]{:S(2)}) collective-permute-start(bf16[32,8192]{1,0:T(8,128)(2,1)} %add_convert_fusion.2), channel_id=1, source_target_pairs={{32,0},{64,32},{96,64},{128,96},{160,128},{192,160},{224,192},{256... | collective-permute-start | bytes 1572872 | tf_op jit(solution)/shard_map/while/body/eval_jaxpr/ppermute | solution.py:13
  422.6 16.6 %collective-permute-start = (bf16[32,8192]{1,0:T(8,128)(2,1)}, bf16[32,8192]{1,0:T(8,128)(2,1)S(1)}, u32[]{:S(2)}, u32[]{:S(2)}) collective-permute-start(bf16[32,8192]{1,0:T(8,128)(2,1)} %add_convert_fusion.2), channel_id=1, source_target_pairs={{32,0},{64,32},{96,64},{128,96},{160,128},{192,160},{224,192},{256... | collective-permute-start | bytes 1572872 | tf_op jit(solution)/shard_map/while/body/eval_jaxpr/ppermute | solution.py:13
  445.9 17.4 %collective-permute-start = (bf16[32,8192]{1,0:T(8,128)(2,1)}, bf16[32,8192]{1,0:T(8,128)(2,1)S(1)}, u32[]{:S(2)}, u32[]{:S(2)}) collective-permute-start(bf16[32,8192]{1,0:T(8,128)(2,1)} %add_convert_fusion.2), channel_id=1, source_target_pairs={{32,0},{64,32},{96,64},{128,96},{160,128},{192,160},{224,192},{256... | collective-permute-start | bytes 1572872 | tf_op jit(solution)/shard_map/while/body/eval_jaxpr/ppermute | solution.py:13
  470.0 18.7 %collective-permute-start = (bf16[32,8192]{1,0:T(8,128)(2,1)}, bf16[32,8192]{1,0:T(8,128)(2,1)S(1)}, u32[]{:S(2)}, u32[]{:S(2)}) collective-permute-start(bf16[32,8192]{1,0:T(8,128)(2,1)} %add_convert_fusion.2), channel_id=1, source_target_pairs={{32,0},{64,32},{96,64},{128,96},{160,128},{192,160},{224,192},{256... | collective-permute-start | bytes 1572872 | tf_op jit(solution)/shard_map/while/body/eval_jaxpr/ppermute | solution.py:13
  495.4 13.3 %collective-permute-start = (bf16[32,8192]{1,0:T(8,128)(2,1)}, bf16[32,8192]{1,0:T(8,128)(2,1)S(1)}, u32[]{:S(2)}, u32[]{:S(2)}) collective-permute-start(bf16[32,8192]{1,0:T(8,128)(2,1)} %add_convert_fusion.2), channel_id=1, source_target_pairs={{32,0},{64,32},{96,64},{128,96},{160,128},{192,160},{224,192},{256... | collective-permute-start | bytes 1572872 | tf_op jit(solution)/shard_map/while/body/eval_jaxpr/ppermute | solution.py:13
  513.6 2.6 copy-start.1
  518.0 149.3 %reduce-scatter.10.cloned.1.call-start = ((), (), s32[]{:S(2)}) async-start(), calls=%async_computation.5 | async-start | bytes 655360
  640.3 58.6 %reduce-scatter.8.cloned.1.call-start = ((), (), s32[]{:S(2)}) async-start(), calls=%async_computation.4 | async-start | bytes 163840 | tf_op jit(solution)/shard_map/reduce_scatter | solution.py:104
  641.9 88.4 %reduce-scatter.6.cloned.1.call-start = ((), (), s32[]{:S(2)}) async-start(), calls=%async_computation.3 | async-start | bytes 163840 | tf_op jit(solution)/shard_map/reduce_scatter | solution.py:103
Sparse Core Ops, SparseCore 0:
  518.2 84.0 all-reduce.2
  640.4 26.9 reduce-scatter.9
  670.7 28.1 reduce-scatter.7
  702.1 28.1 reduce-scatter.5
where the time goes:
time: 741 us; the launch traced here: 738 us
  waiting for transfers between devices  383 us (52%)
  blocking collectives  158 us (21%)
  other arithmetic  96.6 us (13%)
  matrix products  51.7 us (7%)
  starting transfers between devices  24.5 us (3%)
  between operations  17.7 us (2%)
    ppermute x19, waiting for transfers between devices, from_behind(): lax.ppermute(value, axis, [(source, source + steps) for source in range(i...  240 us
    psum x1, waiting for transfers between devices, on_device(): sum_a, sum_b, sum_g = lax.psum((grad_a, grad_b, gain_gradient), 'seq')  57.9 us
    convert_element_type x19, other arithmetic, back_block(): return hidden_gradient.astype(jnp.bfloat16)  43.6 us
    dynamic_update_slice x19, other arithmetic, turn(): lax.dynamic_update_slice_in_dim(mine, jnp.where(inside, source, kept), bl...  42 us
    dot_general x19, matrix products, back_block(): jnp.dot(d_low, a_full, preferred_element_type=jnp.float32)  40.1 us
    all_gather x1, blocking collectives, on_device(): lax.all_gather(a_rows, ('seq', 'dp'), axis=2, tiled=True)  35.9 us
    all_gather x1, blocking collectives, on_device(): lax.all_gather(gain[:, None, :], ('seq', 'dp'), axis=2, tiled=True)  34.2 us
    all_gather x1, blocking collectives, on_device(): lax.all_gather(b_rows, ('seq', 'dp'), axis=2, tiled=True)  32.9 us
  transfers between devices with their start and end apart: 23, of which 23 were waited for; matrix products, arithmetic and copies ran while one was open for 1% of the time, Pallas kernels for 0%

commit v1 on v0

--- a/solution.py
+++ b/solution.py
@@ -19,7 +19,10 @@
     hidden = acts[0, 0]
     top = top_grad[0]
     a_whole, b_whole, gain_whole = (
-        lax.all_gather(a_rows, ("seq", "dp"), axis=2, tiled=True),
+        jnp.concatenate(
+            lax.all_to_all(jnp.stack([a_rows] * lax.axis_size(("seq", "dp"))), ("seq", "dp"), 0, 0),
+            axis=2,
+        ),
         lax.all_gather(b_rows, ("seq", "dp"), axis=2, tiled=True),
         lax.all_gather(gain[:, None, :], ("seq", "dp"), axis=2, tiled=True),
     )

time: 741 us -> 716 us (0.966)
  blocking collectives: 158 us -> 121 us
  starting transfers between devices: 24.5 us -> 33.9 us
    all_gather x1 -> x0, blocking collectives: 35.9 us -> none  [on_device(): lax.all_gather(a_rows, ('seq', 'dp'), axis=2, tiled=True)]
    all_to_all x0 -> x1, starting transfers between devices: none -> 9.38 us  [on_device(): lax.all_to_all(jnp.stack([a_rows] * lax.axis_size(('seq', 'dp'))), ('seq'...]
  transfers between devices with their start and end apart: 23 -> 24, of which waited for: 23 -> 23; matrix products, arithmetic and copies ran while one was open for 1% -> 1% of each run, Pallas kernels for 0% -> 0%
where the time goes in v1:
time: 716 us; the launch traced here: 713 us
  waiting for transfers between devices  387 us (54%)
  blocking collectives  121 us (17%)
  other arithmetic  96.4 us (13%)
  matrix products  50.1 us (7%)
  starting transfers between devices  33.9 us (5%)
  between operations  17.7 us (2%)
  local copies, waits for them, and re-layouts  7.39 us (1%)
    ppermute x19, waiting for transfers between devices, from_behind(): lax.ppermute(value, axis, [(source, source + steps) for source in range(i...  242 us
    psum x1, waiting for transfers between devices, on_device(): sum_a, sum_b, sum_g = lax.psum((grad_a, grad_b, gain_gradient), 'seq')  59.6 us
    convert_element_type x19, other arithmetic, back_block(): return hidden_gradient.astype(jnp.bfloat16)  43.6 us
    dynamic_update_slice x19, other arithmetic, turn(): lax.dynamic_update_slice_in_dim(mine, jnp.where(inside, source, kept), bl...  42 us
    dot_general x19, matrix products, back_block(): jnp.dot(d_low, a_full, preferred_element_type=jnp.float32)  40.1 us
    all_gather x1, blocking collectives, on_device(): lax.all_gather(b_rows, ('seq', 'dp'), axis=2, tiled=True)  33.8 us
    all_gather x1, blocking collectives, on_device(): lax.all_gather(gain[:, None, :], ('seq', 'dp'), axis=2, tiled=True)  31.9 us
    psum x1, blocking collectives, on_device(): total = lax.psum(square, 'pipe')  31.8 us
  transfers between devices with their start and end apart: 24, of which 23 were waited for; matrix products, arithmetic and copies ran while one was open for 1% of the time, Pallas kernels for 0%

profile of v1, /device:TPU:8, one launch (start us, length us, event | category | flops | bytes accessed | tf_op | source)
XLA Modules:
  0.0 713.0 jit_solution(4130603648411270454)
XLA Ops:
  8.9 9.4 %all-to-all-start = ((bf16[32,1,32,256]{3,2,1,0:T(8,128)(2,1)}), bf16[32,1,32,256]{3,2,1,0:T(8,128)(2,1)S(1)}, u32[]{:S(2)}, u32[]{:S(2)}) async-start(bf16[32,1,32,256]{3,2,1,0:T(8,128)(2,1)} %stack.2), calls=%async_computation | async-start | bytes 1048576 | tf_op jit(solution)/shard_map/all_to_all | solution.py:23
  20.5 2.4 fusion.1
  22.9 31.9 %all-gather = bf16[1,8192]{1,0:T(2,128)(2,1)S(1)} all-gather(bf16[1,256]{1,0:T(2,128)(2,1)S(1)} %copy-done.3), channel_id=2, replica_groups=mesh['pipe'=16,'seq'=8,'dp'=4] {'seq','dp'}, dimensions={1}, use_global_device_ids=true | all-gather | bytes 16896 | tf_op jit(solution)/shard_map/all_gather | solution.py:27
  54.8 33.8 %all_gather.6 = bf16[1,32,8192]{2,1,0:T(8,128)(2,1)S(1)} all-gather(bf16[1,32,256]{2,1,0:T(8,128)(2,1)S(1)} %copy-done.2), channel_id=1, replica_groups=mesh['pipe'=16,'seq'=8,'dp'=4] {'seq','dp'}, dimensions={2}, use_global_device_ids=true | all-gather | bytes 540672 | tf_op jit(solution)/shard_map/all_gather | solution.py:26
  90.2 393.6 %while.17 = (s32[]{:T(128)}, bf16[32,8192]{1,0:T(8,128)(2,1)S(1)}, bf16[128,8192]{1,0:T(8,128)(2,1)}, pred[]{:T(512)}, s32[]{:T(128)}, /*index=5*/bf16[128,8192]...) while((s32[]{:T(128)}, bf16[32,8192]{1,0:T(8,128)(2,1)S(1)}, ...), condition=%wide.region_3.4_spmd, body=%wide.region_1.3_spmd.sunk | while | flops 36439052 | bytes 11568829 | solution.py:84
  90.3 2.2 select_dynamic-update-slice_fusion.2
  94.7 2.3 add_convert_fusion.2
  98.3 14.6 %collective-permute-done = bf16[32,8192]{1,0:T(8,128)(2,1)S(1)} collective-permute-done((bf16[32,8192]{1,0:T(8,128)(2,1)}, bf16[32,8192]{1,0:T(8,128)(2,1)S(1)}, u32[]{:S(2)}, u32[]{:S(2)}) %collective-permute-start) | collective-permute-done | bytes 524320 | tf_op jit(solution)/shard_map/while/body/eval_jaxpr/ppermute | solution.py:13
  117.3 2.3 add_convert_fusion.2
  120.9 13.7 %collective-permute-done = bf16[32,8192]{1,0:T(8,128)(2,1)S(1)} collective-permute-done((bf16[32,8192]{1,0:T(8,128)(2,1)}, bf16[32,8192]{1,0:T(8,128)(2,1)S(1)}, u32[]{:S(2)}, u32[]{:S(2)}) %collective-permute-start) | collective-permute-done | bytes 524320 | tf_op jit(solution)/shard_map/while/body/eval_jaxpr/ppermute | solution.py:13
  134.6 2.2 select_dynamic-update-slice_fusion.2
  139.0 2.3 add_convert_fusion.2
  142.6 12.9 %collective-permute-done = bf16[32,8192]{1,0:T(8,128)(2,1)S(1)} collective-permute-done((bf16[32,8192]{1,0:T(8,128)(2,1)}, bf16[32,8192]{1,0:T(8,128)(2,1)S(1)}, u32[]{:S(2)}, u32[]{:S(2)}) %collective-permute-start) | collective-permute-done | bytes 524320 | tf_op jit(solution)/shard_map/while/body/eval_jaxpr/ppermute | solution.py:13
  155.5 2.2 select_dynamic-update-slice_fusion.2
  159.9 2.3 add_convert_fusion.2
  163.4 13.4 %collective-permute-done = bf16[32,8192]{1,0:T(8,128)(2,1)S(1)} collective-permute-done((bf16[32,8192]{1,0:T(8,128)(2,1)}, bf16[32,8192]{1,0:T(8,128)(2,1)S(1)}, u32[]{:S(2)}, u32[]{:S(2)}) %collective-permute-start) | collective-permute-done | bytes 524320 | tf_op jit(solution)/shard_map/while/body/eval_jaxpr/ppermute | solution.py:13
  176.9 2.2 select_dynamic-update-slice_fusion.2
  181.3 2.3 add_convert_fusion.2
  184.9 12.6 %collective-permute-done = bf16[32,8192]{1,0:T(8,128)(2,1)S(1)} collective-permute-done((bf16[32,8192]{1,0:T(8,128)(2,1)}, bf16[32,8192]{1,0:T(8,128)(2,1)S(1)}, u32[]{:S(2)}, u32[]{:S(2)}) %collective-permute-start) | collective-permute-done | bytes 524320 | tf_op jit(solution)/shard_map/while/body/eval_jaxpr/ppermute | solution.py:13
  197.4 2.2 select_dynamic-update-slice_fusion.2
  201.8 2.3 add_convert_fusion.2
  205.4 11.7 %collective-permute-done = bf16[32,8192]{1,0:T(8,128)(2,1)S(1)} collective-permute-done((bf16[32,8192]{1,0:T(8,128)(2,1)}, bf16[32,8192]{1,0:T(8,128)(2,1)S(1)}, u32[]{:S(2)}, u32[]{:S(2)}) %collective-permute-start) | collective-permute-done | bytes 524320 | tf_op jit(solution)/shard_map/while/body/eval_jaxpr/ppermute | solution.py:13
  217.1 2.2 select_dynamic-update-slice_fusion.2
  221.5 2.3 add_convert_fusion.2
  225.1 10.8 %collective-permute-done = bf16[32,8192]{1,0:T(8,128)(2,1)S(1)} collective-permute-done((bf16[32,8192]{1,0:T(8,128)(2,1)}, bf16[32,8192]{1,0:T(8,128)(2,1)S(1)}, u32[]{:S(2)}, u32[]{:S(2)}) %collective-permute-start) | collective-permute-done | bytes 524320 | tf_op jit(solution)/shard_map/while/body/eval_jaxpr/ppermute | solution.py:13
  236.0 2.2 select_dynamic-update-slice_fusion.2
  240.4 2.3 add_convert_fusion.2
  244.0 10.4 %collective-permute-done = bf16[32,8192]{1,0:T(8,128)(2,1)S(1)} collective-permute-done((bf16[32,8192]{1,0:T(8,128)(2,1)}, bf16[32,8192]{1,0:T(8,128)(2,1)S(1)}, u32[]{:S(2)}, u32[]{:S(2)}) %collective-permute-start) | collective-permute-done | bytes 524320 | tf_op jit(solution)/shard_map/while/body/eval_jaxpr/ppermute | solution.py:13
  258.7 2.3 add_convert_fusion.2
  262.3 10.7 %collective-permute-done = bf16[32,8192]{1,0:T(8,128)(2,1)S(1)} collective-permute-done((bf16[32,8192]{1,0:T(8,128)(2,1)}, bf16[32,8192]{1,0:T(8,128)(2,1)S(1)}, u32[]{:S(2)}, u32[]{:S(2)}) %collective-permute-start) | collective-permute-done | bytes 524320 | tf_op jit(solution)/shard_map/while/body/eval_jaxpr/ppermute | solution.py:13
  273.0 2.2 select_dynamic-update-slice_fusion.2
  277.4 2.3 add_convert_fusion.2
  281.0 11.2 %collective-permute-done = bf16[32,8192]{1,0:T(8,128)(2,1)S(1)} collective-permute-done((bf16[32,8192]{1,0:T(8,128)(2,1)}, bf16[32,8192]{1,0:T(8,128)(2,1)S(1)}, u32[]{:S(2)}, u32[]{:S(2)}) %collective-permute-start) | collective-permute-done | bytes 524320 | tf_op jit(solution)/shard_map/while/body/eval_jaxpr/ppermute | solution.py:13
  292.2 2.2 select_dynamic-update-slice_fusion.2
  296.6 2.3 add_convert_fusion.2
  300.2 11.2 %collective-permute-done = bf16[32,8192]{1,0:T(8,128)(2,1)S(1)} collective-permute-done((bf16[32,8192]{1,0:T(8,128)(2,1)}, bf16[32,8192]{1,0:T(8,128)(2,1)S(1)}, u32[]{:S(2)}, u32[]{:S(2)}) %collective-permute-start) | collective-permute-done | bytes 524320 | tf_op jit(solution)/shard_map/while/body/eval_jaxpr/ppermute | solution.py:13
  315.8 2.3 add_convert_fusion.2
  319.4 11.2 %collective-permute-done = bf16[32,8192]{1,0:T(8,128)(2,1)S(1)} collective-permute-done((bf16[32,8192]{1,0:T(8,128)(2,1)}, bf16[32,8192]{1,0:T(8,128)(2,1)S(1)}, u32[]{:S(2)}, u32[]{:S(2)}) %collective-permute-start) | collective-permute-done | bytes 524320 | tf_op jit(solution)/shard_map/while/body/eval_jaxpr/ppermute | solution.py:13
  334.9 2.3 add_convert_fusion.2
  338.5 11.2 %collective-permute-done = bf16[32,8192]{1,0:T(8,128)(2,1)S(1)} collective-permute-done((bf16[32,8192]{1,0:T(8,128)(2,1)}, bf16[32,8192]{1,0:T(8,128)(2,1)S(1)}, u32[]{:S(2)}, u32[]{:S(2)}) %collective-permute-start) | collective-permute-done | bytes 524320 | tf_op jit(solution)/shard_map/while/body/eval_jaxpr/ppermute | solution.py:13
  354.1 2.3 add_convert_fusion.2
  357.7 11.9 %collective-permute-done = bf16[32,8192]{1,0:T(8,128)(2,1)S(1)} collective-permute-done((bf16[32,8192]{1,0:T(8,128)(2,1)}, bf16[32,8192]{1,0:T(8,128)(2,1)S(1)}, u32[]{:S(2)}, u32[]{:S(2)}) %collective-permute-start) | collective-permute-done | bytes 524320 | tf_op jit(solution)/shard_map/while/body/eval_jaxpr/ppermute | solution.py:13
  374.1 2.3 add_convert_fusion.2
  377.7 13.4 %collective-permute-done = bf16[32,8192]{1,0:T(8,128)(2,1)S(1)} collective-permute-done((bf16[32,8192]{1,0:T(8,128)(2,1)}, bf16[32,8192]{1,0:T(8,128)(2,1)S(1)}, u32[]{:S(2)}, u32[]{:S(2)}) %collective-permute-start) | collective-permute-done | bytes 524320 | tf_op jit(solution)/shard_map/while/body/eval_jaxpr/ppermute | solution.py:13
  395.4 2.3 add_convert_fusion.2
  399.0 15.3 %collective-permute-done = bf16[32,8192]{1,0:T(8,128)(2,1)S(1)} collective-permute-done((bf16[32,8192]{1,0:T(8,128)(2,1)}, bf16[32,8192]{1,0:T(8,128)(2,1)S(1)}, u32[]{:S(2)}, u32[]{:S(2)}) %collective-permute-start) | collective-permute-done | bytes 524320 | tf_op jit(solution)/shard_map/while/body/eval_jaxpr/ppermute | solution.py:13
  414.3 2.2 select_dynamic-update-slice_fusion.2
  418.7 2.3 add_convert_fusion.2
  422.3 16.1 %collective-permute-done = bf16[32,8192]{1,0:T(8,128)(2,1)S(1)} collective-permute-done((bf16[32,8192]{1,0:T(8,128)(2,1)}, bf16[32,8192]{1,0:T(8,128)(2,1)S(1)}, u32[]{:S(2)}, u32[]{:S(2)}) %collective-permute-start) | collective-permute-done | bytes 524320 | tf_op jit(solution)/shard_map/while/body/eval_jaxpr/ppermute | solution.py:13
  438.4 2.2 select_dynamic-update-slice_fusion.2
  442.8 2.3 add_convert_fusion.2
  446.4 17.4 %collective-permute-done = bf16[32,8192]{1,0:T(8,128)(2,1)S(1)} collective-permute-done((bf16[32,8192]{1,0:T(8,128)(2,1)}, bf16[32,8192]{1,0:T(8,128)(2,1)S(1)}, u32[]{:S(2)}, u32[]{:S(2)}) %collective-permute-start) | collective-permute-done | bytes 524320 | tf_op jit(solution)/shard_map/while/body/eval_jaxpr/ppermute | solution.py:13
  463.8 2.2 select_dynamic-update-slice_fusion.2
  468.2 2.3 add_convert_fusion.2
  471.8 12.0 %collective-permute-done = bf16[32,8192]{1,0:T(8,128)(2,1)S(1)} collective-permute-done((bf16[32,8192]{1,0:T(8,128)(2,1)}, bf16[32,8192]{1,0:T(8,128)(2,1)S(1)}, u32[]{:S(2)}, u32[]{:S(2)}) %collective-permute-start) | collective-permute-done | bytes 524320 | tf_op jit(solution)/shard_map/while/body/eval_jaxpr/ppermute | solution.py:13
  483.8 4.9 fusion.16
  488.8 2.5 convolution_convert_fusion.1
  494.0 23.1 %psum.30 = f32[1,8192]{1,0:T(1,128)S(1)} all-reduce(f32[1,8192]{1,0:T(1,128)S(1)} %bitcast.67), channel_id=1, replica_groups=mesh['pipe'=16,'seq'=8,'dp'=4] {'seq'}, use_global_device_ids=true, to_apply=%region_9.10 | all-reduce | flops 8192 | bytes 65536 | tf_op jit(solution)/shard_map/psum | solution.py:95
  517.7 59.6 %all-reduce.3.cloned.1.call-done = (f32[32,8192]{1,0:T(8,128)}, f32[32,8192]{1,0:T(8,128)}) async-done(((f32[32,8192]{1,0:T(8,128)}, f32[32,8192]{1,0:T(8,128)}), (f32[32,8192]{1,0:T(8,128)}, f32[32,8192]{1,0:T(8,128)})) %all-reduce.3.cloned.1.call-update) | async-done | bytes 2097168 | tf_op jit(solution)/shard_map/psum | solution.py:95
  577.4 2.4 multiply_reduce_fusion.1
  581.7 31.8 %psum.31 = f32[]{:T(128)} all-reduce(f32[]{:T(128)S(6)} %add.88), channel_id=1, replica_groups=mesh['pipe'=16,'seq'=8,'dp'=4] {'pipe'}, use_global_device_ids=true, to_apply=%region_11.12 | all-reduce | flops 1 | bytes 8 | tf_op jit(solution)/shard_map/psum | solution.py:97
  618.6 23.8 %reduce-scatter.10.cloned.1.call-done = f32[256,1]{1,0:T(8,128)} async-done(((f32[1024,1]{1,0:T(8,128)}), f32[256,1]{1,0:T(8,128)}) %reduce-scatter.10.cloned.1.call-update) | async-done | bytes 1040
  644.0 30.0 %reduce-scatter.8.cloned.1.call-done = f32[32,256]{1,0:T(8,128)} async-done(((f32[32,1024]{1,0:T(8,128)}), f32[32,256]{1,0:T(8,128)}) %reduce-scatter.8.cloned.1.call-update) | async-done | bytes 32784 | tf_op jit(solution)/shard_map/reduce_scatter | solution.py:107
  674.0 31.4 %reduce-scatter.6.cloned.1.call-done = f32[32,256]{1,0:T(8,128)} async-done(((f32[32,1024]{1,0:T(8,128)}), f32[32,256]{1,0:T(8,128)}) %reduce-scatter.6.cloned.1.call-update) | async-done | bytes 32784 | tf_op jit(solution)/shard_map/reduce_scatter | solution.py:106
  (115 shorter events, 96.1 us)
Async XLA Ops:
  7.2 13.3 %copy-start = (bf16[1,1,128,8192]{3,2,1,0:T(8,128)(2,1)S(1)}, bf16[1,1,128,8192]{3,2,1,0:T(8,128)(2,1)}, u32[]{:S(2)}) copy-start(bf16[1,1,128,8192]{3,2,1,0:T(8,128)(2,1)} %param.7) | copy-start | bytes 6291460
  8.9 79.7 %all-to-all-start = ((bf16[32,1,32,256]{3,2,1,0:T(8,128)(2,1)}), bf16[32,1,32,256]{3,2,1,0:T(8,128)(2,1)S(1)}, u32[]{:S(2)}, u32[]{:S(2)}) async-start(bf16[32,1,32,256]{3,2,1,0:T(8,128)(2,1)} %stack.2), calls=%async_computation | async-start | bytes 1048576 | tf_op jit(solution)/shard_map/all_to_all | solution.py:23
  18.3 559.1 %all-reduce.3.cloned.1.call-start = ((), (), s32[]{:S(2)}) async-start(), calls=%async_computation.7 | async-start | bytes 4194304 | tf_op jit(solution)/shard_map/psum | solution.py:95
  20.4 2.4 copy-start.3
  20.4 34.4 %copy-start.2 = (bf16[1,32,256]{2,1,0:T(8,128)(2,1)S(1)}, bf16[1,32,256]{2,1,0:T(8,128)(2,1)}, u32[]{:S(2)}) copy-start(bf16[1,32,256]{2,1,0:T(8,128)(2,1)} %param.10) | copy-start | bytes 49156
  97.0 15.9 %collective-permute-start = (bf16[32,8192]{1,0:T(8,128)(2,1)}, bf16[32,8192]{1,0:T(8,128)(2,1)S(1)}, u32[]{:S(2)}, u32[]{:S(2)}) collective-permute-start(bf16[32,8192]{1,0:T(8,128)(2,1)} %add_convert_fusion.2), channel_id=1, source_target_pairs={{32,0},{64,32},{96,64},{128,96},{160,128},{192,160},{224,192},{256... | collective-permute-start | bytes 1572872 | tf_op jit(solution)/shard_map/while/body/eval_jaxpr/ppermute | solution.py:13
  119.6 15.0 %collective-permute-start = (bf16[32,8192]{1,0:T(8,128)(2,1)}, bf16[32,8192]{1,0:T(8,128)(2,1)S(1)}, u32[]{:S(2)}, u32[]{:S(2)}) collective-permute-start(bf16[32,8192]{1,0:T(8,128)(2,1)} %add_convert_fusion.2), channel_id=1, source_target_pairs={{32,0},{64,32},{96,64},{128,96},{160,128},{192,160},{224,192},{256... | collective-permute-start | bytes 1572872 | tf_op jit(solution)/shard_map/while/body/eval_jaxpr/ppermute | solution.py:13
  141.3 14.2 %collective-permute-start = (bf16[32,8192]{1,0:T(8,128)(2,1)}, bf16[32,8192]{1,0:T(8,128)(2,1)S(1)}, u32[]{:S(2)}, u32[]{:S(2)}) collective-permute-start(bf16[32,8192]{1,0:T(8,128)(2,1)} %add_convert_fusion.2), channel_id=1, source_target_pairs={{32,0},{64,32},{96,64},{128,96},{160,128},{192,160},{224,192},{256... | collective-permute-start | bytes 1572872 | tf_op jit(solution)/shard_map/while/body/eval_jaxpr/ppermute | solution.py:13
  162.2 14.7 %collective-permute-start = (bf16[32,8192]{1,0:T(8,128)(2,1)}, bf16[32,8192]{1,0:T(8,128)(2,1)S(1)}, u32[]{:S(2)}, u32[]{:S(2)}) collective-permute-start(bf16[32,8192]{1,0:T(8,128)(2,1)} %add_convert_fusion.2), channel_id=1, source_target_pairs={{32,0},{64,32},{96,64},{128,96},{160,128},{192,160},{224,192},{256... | collective-permute-start | bytes 1572872 | tf_op jit(solution)/shard_map/while/body/eval_jaxpr/ppermute | solution.py:13
  183.6 13.9 %collective-permute-start = (bf16[32,8192]{1,0:T(8,128)(2,1)}, bf16[32,8192]{1,0:T(8,128)(2,1)S(1)}, u32[]{:S(2)}, u32[]{:S(2)}) collective-permute-start(bf16[32,8192]{1,0:T(8,128)(2,1)} %add_convert_fusion.2), channel_id=1, source_target_pairs={{32,0},{64,32},{96,64},{128,96},{160,128},{192,160},{224,192},{256... | collective-permute-start | bytes 1572872 | tf_op jit(solution)/shard_map/while/body/eval_jaxpr/ppermute | solution.py:13
  204.1 13.0 %collective-permute-start = (bf16[32,8192]{1,0:T(8,128)(2,1)}, bf16[32,8192]{1,0:T(8,128)(2,1)S(1)}, u32[]{:S(2)}, u32[]{:S(2)}) collective-permute-start(bf16[32,8192]{1,0:T(8,128)(2,1)} %add_convert_fusion.2), channel_id=1, source_target_pairs={{32,0},{64,32},{96,64},{128,96},{160,128},{192,160},{224,192},{256... | collective-permute-start | bytes 1572872 | tf_op jit(solution)/shard_map/while/body/eval_jaxpr/ppermute | solution.py:13
  223.8 12.1 %collective-permute-start = (bf16[32,8192]{1,0:T(8,128)(2,1)}, bf16[32,8192]{1,0:T(8,128)(2,1)S(1)}, u32[]{:S(2)}, u32[]{:S(2)}) collective-permute-start(bf16[32,8192]{1,0:T(8,128)(2,1)} %add_convert_fusion.2), channel_id=1, source_target_pairs={{32,0},{64,32},{96,64},{128,96},{160,128},{192,160},{224,192},{256... | collective-permute-start | bytes 1572872 | tf_op jit(solution)/shard_map/while/body/eval_jaxpr/ppermute | solution.py:13
  242.7 11.6 %collective-permute-start = (bf16[32,8192]{1,0:T(8,128)(2,1)}, bf16[32,8192]{1,0:T(8,128)(2,1)S(1)}, u32[]{:S(2)}, u32[]{:S(2)}) collective-permute-start(bf16[32,8192]{1,0:T(8,128)(2,1)} %add_convert_fusion.2), channel_id=1, source_target_pairs={{32,0},{64,32},{96,64},{128,96},{160,128},{192,160},{224,192},{256... | collective-permute-start | bytes 1572872 | tf_op jit(solution)/shard_map/while/body/eval_jaxpr/ppermute | solution.py:13
  261.0 12.0 %collective-permute-start = (bf16[32,8192]{1,0:T(8,128)(2,1)}, bf16[32,8192]{1,0:T(8,128)(2,1)S(1)}, u32[]{:S(2)}, u32[]{:S(2)}) collective-permute-start(bf16[32,8192]{1,0:T(8,128)(2,1)} %add_convert_fusion.2), channel_id=1, source_target_pairs={{32,0},{64,32},{96,64},{128,96},{160,128},{192,160},{224,192},{256... | collective-permute-start | bytes 1572872 | tf_op jit(solution)/shard_map/while/body/eval_jaxpr/ppermute | solution.py:13
  279.7 12.5 %collective-permute-start = (bf16[32,8192]{1,0:T(8,128)(2,1)}, bf16[32,8192]{1,0:T(8,128)(2,1)S(1)}, u32[]{:S(2)}, u32[]{:S(2)}) collective-permute-start(bf16[32,8192]{1,0:T(8,128)(2,1)} %add_convert_fusion.2), channel_id=1, source_target_pairs={{32,0},{64,32},{96,64},{128,96},{160,128},{192,160},{224,192},{256... | collective-permute-start | bytes 1572872 | tf_op jit(solution)/shard_map/while/body/eval_jaxpr/ppermute | solution.py:13
  298.9 12.5 %collective-permute-start = (bf16[32,8192]{1,0:T(8,128)(2,1)}, bf16[32,8192]{1,0:T(8,128)(2,1)S(1)}, u32[]{:S(2)}, u32[]{:S(2)}) collective-permute-start(bf16[32,8192]{1,0:T(8,128)(2,1)} %add_convert_fusion.2), channel_id=1, source_target_pairs={{32,0},{64,32},{96,64},{128,96},{160,128},{192,160},{224,192},{256... | collective-permute-start | bytes 1572872 | tf_op jit(solution)/shard_map/while/body/eval_jaxpr/ppermute | solution.py:13
  318.1 12.5 %collective-permute-start = (bf16[32,8192]{1,0:T(8,128)(2,1)}, bf16[32,8192]{1,0:T(8,128)(2,1)S(1)}, u32[]{:S(2)}, u32[]{:S(2)}) collective-permute-start(bf16[32,8192]{1,0:T(8,128)(2,1)} %add_convert_fusion.2), channel_id=1, source_target_pairs={{32,0},{64,32},{96,64},{128,96},{160,128},{192,160},{224,192},{256... | collective-permute-start | bytes 1572872 | tf_op jit(solution)/shard_map/while/body/eval_jaxpr/ppermute | solution.py:13
  337.2 12.5 %collective-permute-start = (bf16[32,8192]{1,0:T(8,128)(2,1)}, bf16[32,8192]{1,0:T(8,128)(2,1)S(1)}, u32[]{:S(2)}, u32[]{:S(2)}) collective-permute-start(bf16[32,8192]{1,0:T(8,128)(2,1)} %add_convert_fusion.2), channel_id=1, source_target_pairs={{32,0},{64,32},{96,64},{128,96},{160,128},{192,160},{224,192},{256... | collective-permute-start | bytes 1572872 | tf_op jit(solution)/shard_map/while/body/eval_jaxpr/ppermute | solution.py:13
  356.4 13.2 %collective-permute-start = (bf16[32,8192]{1,0:T(8,128)(2,1)}, bf16[32,8192]{1,0:T(8,128)(2,1)S(1)}, u32[]{:S(2)}, u32[]{:S(2)}) collective-permute-start(bf16[32,8192]{1,0:T(8,128)(2,1)} %add_convert_fusion.2), channel_id=1, source_target_pairs={{32,0},{64,32},{96,64},{128,96},{160,128},{192,160},{224,192},{256... | collective-permute-start | bytes 1572872 | tf_op jit(solution)/shard_map/while/body/eval_jaxpr/ppermute | solution.py:13
  376.4 14.7 %collective-permute-start = (bf16[32,8192]{1,0:T(8,128)(2,1)}, bf16[32,8192]{1,0:T(8,128)(2,1)S(1)}, u32[]{:S(2)}, u32[]{:S(2)}) collective-permute-start(bf16[32,8192]{1,0:T(8,128)(2,1)} %add_convert_fusion.2), channel_id=1, source_target_pairs={{32,0},{64,32},{96,64},{128,96},{160,128},{192,160},{224,192},{256... | collective-permute-start | bytes 1572872 | tf_op jit(solution)/shard_map/while/body/eval_jaxpr/ppermute | solution.py:13
  397.7 16.6 %collective-permute-start = (bf16[32,8192]{1,0:T(8,128)(2,1)}, bf16[32,8192]{1,0:T(8,128)(2,1)S(1)}, u32[]{:S(2)}, u32[]{:S(2)}) collective-permute-start(bf16[32,8192]{1,0:T(8,128)(2,1)} %add_convert_fusion.2), channel_id=1, source_target_pairs={{32,0},{64,32},{96,64},{128,96},{160,128},{192,160},{224,192},{256... | collective-permute-start | bytes 1572872 | tf_op jit(solution)/shard_map/while/body/eval_jaxpr/ppermute | solution.py:13
  421.0 17.4 %collective-permute-start = (bf16[32,8192]{1,0:T(8,128)(2,1)}, bf16[32,8192]{1,0:T(8,128)(2,1)S(1)}, u32[]{:S(2)}, u32[]{:S(2)}) collective-permute-start(bf16[32,8192]{1,0:T(8,128)(2,1)} %add_convert_fusion.2), channel_id=1, source_target_pairs={{32,0},{64,32},{96,64},{128,96},{160,128},{192,160},{224,192},{256... | collective-permute-start | bytes 1572872 | tf_op jit(solution)/shard_map/while/body/eval_jaxpr/ppermute | solution.py:13
  445.1 18.7 %collective-permute-start = (bf16[32,8192]{1,0:T(8,128)(2,1)}, bf16[32,8192]{1,0:T(8,128)(2,1)S(1)}, u32[]{:S(2)}, u32[]{:S(2)}) collective-permute-start(bf16[32,8192]{1,0:T(8,128)(2,1)} %add_convert_fusion.2), channel_id=1, source_target_pairs={{32,0},{64,32},{96,64},{128,96},{160,128},{192,160},{224,192},{256... | collective-permute-start | bytes 1572872 | tf_op jit(solution)/shard_map/while/body/eval_jaxpr/ppermute | solution.py:13
  470.5 13.3 %collective-permute-start = (bf16[32,8192]{1,0:T(8,128)(2,1)}, bf16[32,8192]{1,0:T(8,128)(2,1)S(1)}, u32[]{:S(2)}, u32[]{:S(2)}) collective-permute-start(bf16[32,8192]{1,0:T(8,128)(2,1)} %add_convert_fusion.2), channel_id=1, source_target_pairs={{32,0},{64,32},{96,64},{128,96},{160,128},{192,160},{224,192},{256... | collective-permute-start | bytes 1572872 | tf_op jit(solution)/shard_map/while/body/eval_jaxpr/ppermute | solution.py:13
  488.8 2.6 copy-start.1
  493.2 149.3 %reduce-scatter.10.cloned.1.call-start = ((), (), s32[]{:S(2)}) async-start(), calls=%async_computation.6 | async-start | bytes 655360
  615.3 58.6 %reduce-scatter.8.cloned.1.call-start = ((), (), s32[]{:S(2)}) async-start(), calls=%async_computation.5 | async-start | bytes 163840 | tf_op jit(solution)/shard_map/reduce_scatter | solution.py:107
  617.0 88.4 %reduce-scatter.6.cloned.1.call-start = ((), (), s32[]{:S(2)}) async-start(), calls=%async_computation.4 | async-start | bytes 163840 | tf_op jit(solution)/shard_map/reduce_scatter | solution.py:106
Sparse Core Ops, SparseCore 0:
  493.3 84.0 all-reduce.2
  615.5 26.9 reduce-scatter.9
  645.8 28.1 reduce-scatter.7
  677.2 28.1 reduce-scatter.5
